TPU v7x, 128 devices: a whole 4x4x4 slice. The times are simulated.
128 devices in a mesh: node: 4 (over z), local: 32 (over x, y, core).
Axes of the slice: x: 4, y: 4, z: 4, core: 2. Of those that a mesh axis runs over, the one named last changes fastest.
Arguments:
- tokens: bfloat16 [16384, 3584], P(('node', 'local')), may hold values from -6 to 6
- group_ids: int32 [16384, 2], P(('node', 'local')), may hold values from 0 to 3, as said below
- local_ids: int32 [16384, 8], P(('node', 'local')), may hold values from 0 to 31, as said below
- router: bfloat16 [3584, 128], replicated, may hold values from -0.09375 to 0.09375
- w_gate: bfloat16 [128, 3584, 1024], P(('node', 'local')), may hold values from -0.09375 to 0.09375
- w_up: bfloat16 [128, 3584, 1024], P(('node', 'local')), may hold values from -0.09375 to 0.09375
- w_down: bfloat16 [128, 1024, 3584], P(('node', 'local')), may hold values from -0.1875 to 0.1875
Outputs:
- moe_out: bfloat16 [16384, 3584], P(('node', 'local'))
Inputs may be any that keep to these rules, and one draw needn't show every extreme that they name: `group_ids`: each token names two different node groups; the tokens of one device name every node group exactly 64 times. `local_ids`: entry k names an expert of node group group_ids[t, k // 4]; the four entries of one group are different. The tokens of one device route at most 10 tokens to one expert, and in every node group some expert receives exactly 10 tokens from every device.
All inputs are finite; a program needn't handle non-finite values.
Results may differ from a plain program's by a relative error of at most 0.0058.
Values may be sent and summed in bfloat16 or wider, within the bound.
No kernel may reach another device: no remote copies, remote signals or barrier semaphores. Data moves between devices by JAX's collectives and lax.ppermute only.
A program may use at most 128 MiB of HBM per device.

v0:
```python
import jax
import jax.numpy as jnp
from jax import lax
from jax.sharding import PartitionSpec as P


def slot_positions(targets, bins):
    onehot = (targets[:, None] == jnp.arange(bins, dtype=jnp.int32)[None, :]).astype(jnp.int32)
    earlier = jnp.cumsum(onehot, axis=0) - onehot
    return jnp.sum(earlier * onehot, axis=1)


def fill_slots(source_rows, owners, slot_index, slot_total):
    src_table = jnp.full((slot_total,), source_rows.shape[0], jnp.int32).at[slot_index].set(owners)
    padded = jnp.concatenate(
        [source_rows, jnp.zeros((1, source_rows.shape[1]), source_rows.dtype)], axis=0
    )
    return padded[src_table]


def expert_rows(flat_rows, w_gate, w_up, w_down):
    gate_part = jnp.dot(flat_rows, w_gate[0], preferred_element_type=jnp.float32)
    up_part = jnp.dot(flat_rows, w_up[0], preferred_element_type=jnp.float32)
    hidden = (jax.nn.silu(gate_part) * up_part).astype(jnp.bfloat16)
    return jnp.dot(hidden, w_down[0], preferred_element_type=jnp.float32).astype(jnp.bfloat16)


def on_device(tokens, group_ids, local_ids, router, w_gate, w_up, w_down):
    tok_dev, feat_width = tokens.shape
    node_size = lax.axis_size("node")
    local_size = lax.axis_size("local")
    experts_all = node_size * local_size
    cap_rows = 5 * tok_dev // (2 * local_size)
    group_count = group_ids.shape[1]
    per_group = local_ids.shape[1] // group_count
    expert_ids = jnp.repeat(group_ids, per_group, axis=1) * local_size + local_ids
    affinity = jax.nn.sigmoid(jnp.dot(tokens, router, preferred_element_type=jnp.float32))
    picked = jnp.take_along_axis(affinity, expert_ids, axis=1)
    picked_total = jnp.sum(picked, axis=1)
    flat_ids = expert_ids.reshape(-1)
    slot_index = flat_ids * cap_rows + slot_positions(flat_ids, experts_all)
    owners = jnp.arange(flat_ids.shape[0], dtype=jnp.int32) // local_ids.shape[1]
    send_rows = fill_slots(tokens, owners, slot_index, experts_all * cap_rows).reshape(
        experts_all, cap_rows, feat_width
    )
    received = lax.all_to_all(send_rows, ("node", "local"), split_axis=0, concat_axis=0, tiled=True)
    lead_size, item_count, _ = received.shape
    produced = expert_rows(received.reshape(-1, feat_width), w_gate, w_up, w_down).reshape(
        lead_size, item_count, feat_width
    )
    returned = lax.all_to_all(produced, ("node", "local"), split_axis=0, concat_axis=0, tiled=True)
    expert_terms = returned.reshape(-1, feat_width)[slot_index].reshape(tok_dev, -1, feat_width)
    weights = 2.5 * picked / picked_total[:, None]
    mixed = jnp.sum(weights[:, :, None] * expert_terms.astype(jnp.float32), axis=1)
    return mixed.astype(jnp.bfloat16)


def solution(mesh):
    return jax.shard_map(
        on_device,
        mesh=mesh,
        in_specs=(
            P(("node", "local"), None),
            P(("node", "local"), None),
            P(("node", "local"), None),
            P(),
            P(("node", "local"), None, None),
            P(("node", "local"), None, None),
            P(("node", "local"), None, None),
        ),
        out_specs=P(("node", "local"), None),
        check_vma=False,
    )
```

profile of v0, /device:TPU:14, one launch (start us, length us, event | category | flops | bytes accessed | tf_op | source)
XLA Modules:
  0.0 512.8 jit_solution(7502446827246861356)
XLA Ops:
  0.0 0.8 broadcast_multiply_fusion.1
  0.8 0.7 bitcast_or_fusion
  1.5 0.1 copy.17
  1.6 0.1 eq.29
  1.7 0.1 eq.25
  1.8 0.1 copy.19
  1.9 0.2 fusion.13
  2.2 0.1 copy.20
  2.3 0.1 copy.16
  2.4 0.1 mul.60
  2.5 0.4 fusion.12
  2.9 4.3 scatter_custom_fusion
  7.2 1.2 concatenate.3
  8.5 7.8 %gather_fusion = bf16[1280,3584]{1,0:T(8,128)(2,1)} fusion(bf16[129,3584]{1,0:T(8,128)(2,1)S(1)} %concatenate.3, s32[2048]{0:T(1024)S(1)} %pad_clamp_fusion), kind=kCustom, calls=%fused_computation | custom fusion | bytes 18355200 | tf_op jit(solution)/shard_map/gather | solution.py:18
  16.3 14.2 %reshape.87 = bf16[128,10,3584]{2,1,0:T(8,128)(2,1)} reshape(bf16[1280,3584]{1,0:T(8,128)(2,1)} %gather_fusion) | data formatting | bytes 18350080 | tf_op jit(solution)/shard_map/reshape | solution.py:43
  30.5 173.6 %all_to_all.10 = bf16[128,10,3584]{2,1,0:T(8,128)(2,1)} all-to-all(bf16[128,10,3584]{2,1,0:T(8,128)(2,1)} %reshape.87), channel_id=1, replica_groups=mesh['node'=4,'local'=32] {'node','local'}, dimensions={0} | all-to-all | bytes 18350080 | tf_op jit(solution)/shard_map/all_to_all | solution.py:46
  204.1 14.7 %reshape.88 = bf16[1280,3584]{1,0:T(8,128)(2,1)} reshape(bf16[128,10,3584]{2,1,0:T(8,128)(2,1)} %all_to_all.10) | data formatting | bytes 18350080 | tf_op jit(solution)/shard_map/reshape | solution.py:48
  218.8 13.4 %fusion.2 = f32[1280,1024]{1,0:T(8,128)S(1)} fusion(bf16[1280,3584]{1,0:T(8,128)(2,1)} %reshape.88, bf16[1,3584,1024]{2,1,0:T(8,128)(2,1)} %param.12), kind=kOutput, calls=%fused_computation.8 | convolution fusion | flops 9395240960 | bytes 21757952 | tf_op jit(solution)/shard_map/dot_general | solution.py:23
  232.2 12.7 %multiply_convert_fusion = bf16[1280,1024]{1,0:T(8,128)(2,1)S(1)} fusion(f32[1280,1024]{1,0:T(8,128)S(1)} %fusion.2, bf16[1280,3584]{1,0:T(8,128)(2,1)S(1)} %copy-done.1, bf16[1,3584,1024]{2,1,0:T(8,128)(2,1)} %param.11), kind=kOutput, calls=%fused_computation.12 | convolution fusion | flops 9403105280 | bytes 24379392 | tf_op jit(solution)/shard_map/dot_general | solution.py:22
  245.0 14.9 %convolution_convert_fusion = bf16[1280,3584]{1,0:T(8,128)(2,1)} fusion(bf16[1280,1024]{1,0:T(8,128)(2,1)S(1)} %multiply_convert_fusion, bf16[1,1024,3584]{2,1,0:T(8,128)(2,1)} %param.13), kind=kOutput, calls=%fused_computation.4 | convolution fusion | flops 9399828480 | bytes 19136512 | tf_op jit(solution)/shard_map/dot_general | solution.py:25
  259.9 14.2 %reshape.89 = bf16[128,10,3584]{2,1,0:T(8,128)(2,1)} reshape(bf16[1280,3584]{1,0:T(8,128)(2,1)} %convolution_convert_fusion) | data formatting | bytes 18350080 | tf_op jit(solution)/shard_map/reshape | solution.py:48
  274.1 8.0 %all-to-all-start.1 = ((bf16[128,10,3584]{2,1,0:T(8,128)(2,1)}), bf16[128,10,3584]{2,1,0:T(8,128)(2,1)}, u32[]{:S(2)}, u32[]{:S(2)}) async-start(bf16[128,10,3584]{2,1,0:T(8,128)(2,1)} %reshape.89), calls=%async_computation.1 | async-start | bytes 29360128 | tf_op jit(solution)/shard_map/all_to_all | solution.py:51
  282.2 0.1 copy.13
  282.3 0.1 reshape.108
  282.4 0.4 fusion.10
  282.8 6.8 %gather_fusion.2 = f32[1024]{0:T(1024)S(1)} fusion(f32[128,128]{1,0:T(8,128)S(1)} %fusion.10, s32[1024]{0:T(1024)S(1)} %reshape.108), kind=kCustom, calls=%fused_computation.2 | custom fusion | bytes 16384 | tf_op jit(solution)/shard_map/jit(take_along_axis)/gather | solution.py:38
  289.6 0.1 reshape.111
  289.8 0.1 copy.15
  289.9 179.0 %all-to-all-done.1 = bf16[128,10,3584]{2,1,0:T(8,128)(2,1)} async-done(((bf16[128,10,3584]{2,1,0:T(8,128)(2,1)}), bf16[128,10,3584]{2,1,0:T(8,128)(2,1)}, u32[]{:S(2)}, u32[]{:S(2)}) %all-to-all-start.1) | async-done | bytes 9175072 | tf_op jit(solution)/shard_map/all_to_all | solution.py:51
  468.9 14.6 %reshape.90 = bf16[1280,3584]{1,0:T(8,128)(2,1)} reshape(bf16[128,10,3584]{2,1,0:T(8,128)(2,1)} %all-to-all-done.1) | data formatting | bytes 18350080 | tf_op jit(solution)/shard_map/reshape | solution.py:52
  483.5 18.6 %gather_fusion.1 = bf16[1024,3584]{1,0:T(8,128)(2,1)} fusion(bf16[1280,3584]{1,0:T(8,128)(2,1)} %reshape.90, s32[1024]{0:T(1024)S(1)} %broadcast_clamp_fusion), kind=kCustom, calls=%fused_computation.1 | custom fusion | bytes 14684160 | tf_op jit(solution)/shard_map/gather | solution.py:52
  502.1 10.7 %fusion = bf16[128,3584]{1,0:T(8,128)(2,1)} fusion(bf16[1024,3584]{1,0:T(8,128)(2,1)} %gather_fusion.1, f32[128,8]{1,0:T(8,128)S(1)} %copy.15), kind=kLoop, calls=%fused_computation.6 | loop fusion | flops 10551296 | bytes 8261632 | tf_op jit(solution)/shard_map/reduce_sum | solution.py:54
  (20 shorter events, 0.2 us)
Async XLA Ops:
  0.0 282.4 %copy-start = (bf16[3584,128]{1,0:T(8,128)(2,1)S(1)}, bf16[3584,128]{1,0:T(8,128)(2,1)}, u32[]{:S(2)}) copy-start(bf16[3584,128]{1,0:T(8,128)(2,1)} %param.10) | copy-start | bytes 2752516
  218.8 13.5 %copy-start.1 = (bf16[1280,3584]{1,0:T(8,128)(2,1)S(1)}, bf16[1280,3584]{1,0:T(8,128)(2,1)}, u32[]{:S(2)}) copy-start(bf16[1280,3584]{1,0:T(8,128)(2,1)} %reshape.88) | copy-start | bytes 27525124
  274.1 8.3 %copy-start.2 = (bf16[128,3584]{1,0:T(8,128)(2,1)S(1)}, bf16[128,3584]{1,0:T(8,128)(2,1)}, u32[]{:S(2)}) copy-start(bf16[128,3584]{1,0:T(8,128)(2,1)} %param.7) | copy-start | bytes 2752516
  274.1 194.8 %all-to-all-start.1 = ((bf16[128,10,3584]{2,1,0:T(8,128)(2,1)}), bf16[128,10,3584]{2,1,0:T(8,128)(2,1)}, u32[]{:S(2)}, u32[]{:S(2)}) async-start(bf16[128,10,3584]{2,1,0:T(8,128)(2,1)} %reshape.89), calls=%async_computation.1 | async-start | bytes 29360128 | tf_op jit(solution)/shard_map/all_to_all | solution.py:51
where the time goes:
time: 521 us; the launch traced here: 513 us
  waiting for transfers between devices  179 us (34%)
  blocking collectives  174 us (33%)
  local copies, waits for them, and re-layouts  97.6 us (19%)
  matrix products  41.5 us (8%)
  other arithmetic  12.9 us (2%)
  starting transfers between devices  8.04 us (2%)
    all_to_all x1, waiting for transfers between devices, on_device(): lax.all_to_all(produced, ('node', 'local'), split_axis=0, concat_axis=0,...  179 us
    all_to_all x1, blocking collectives, on_device(): lax.all_to_all(send_rows, ('node', 'local'), split_axis=0, concat_axis=0,...  174 us
    gather x1, local copies, waits for them, and re-layouts, on_device(): returned.reshape(-1, feat_width)[slot_index]  18.6 us
    dot_general x1, matrix products, expert_rows(): jnp.dot(hidden, w_down[0], preferred_element_type=jnp.float32)  14.9 us
    reshape x1, local copies, waits for them, and re-layouts, on_device(): received.reshape(-1, feat_width)  14.7 us
    reshape x1, local copies, waits for them, and re-layouts, on_device(): returned.reshape(-1, feat_width)[slot_index]  14.6 us
    reshape x1, local copies, waits for them, and re-layouts, on_device(): expert_rows(received.reshape(-1, feat_width), w_gate, w_up, w_down)  14.2 us
    reshape x1, local copies, waits for them, and re-layouts, on_device(): fill_slots(tokens, owners, slot_index, experts_all * cap_rows)  14.2 us
  transfers between devices with their start and end apart: 1, of which 1 were waited for; matrix products, arithmetic and copies ran while one was open for 1% of the time, Pallas kernels for 0%

commit v1 on v0

--- a/solution.py
+++ b/solution.py
@@ -2,6 +2,8 @@
 import jax.numpy as jnp
 from jax import lax
 from jax.sharding import PartitionSpec as P
+
+LANES = 128
 
 
 def slot_positions(targets, bins):
@@ -40,14 +42,10 @@
     flat_ids = expert_ids.reshape(-1)
     slot_index = flat_ids * cap_rows + slot_positions(flat_ids, experts_all)
     owners = jnp.arange(flat_ids.shape[0], dtype=jnp.int32) // local_ids.shape[1]
-    send_rows = fill_slots(tokens, owners, slot_index, experts_all * cap_rows).reshape(
-        experts_all, cap_rows, feat_width
-    )
+    wire = (experts_all, cap_rows * feat_width // LANES, LANES)
+    send_rows = fill_slots(tokens, owners, slot_index, experts_all * cap_rows).reshape(wire)
     received = lax.all_to_all(send_rows, ("node", "local"), split_axis=0, concat_axis=0, tiled=True)
-    lead_size, item_count, _ = received.shape
-    produced = expert_rows(received.reshape(-1, feat_width), w_gate, w_up, w_down).reshape(
-        lead_size, item_count, feat_width
-    )
+    produced = expert_rows(received.reshape(-1, feat_width), w_gate, w_up, w_down).reshape(wire)
     returned = lax.all_to_all(produced, ("node", "local"), split_axis=0, concat_axis=0, tiled=True)
     expert_terms = returned.reshape(-1, feat_width)[slot_index].reshape(tok_dev, -1, feat_width)
     weights = 2.5 * picked / picked_total[:, None]

time: 521 us -> 390 us (0.75)
  waiting for transfers between devices: 179 us -> 101 us
  blocking collectives: 174 us -> 115 us
  local copies, waits for them, and re-layouts: 97.6 us -> 109 us
    all_to_all x1, waiting for transfers between devices: 179 us -> 101 us  [on_device(): lax.all_to_all(produced, ('node', 'local'), split_axis=0, concat_axis=0,...]
    all_to_all x1, blocking collectives: 174 us -> 115 us  [on_device(): lax.all_to_all(send_rows, ('node', 'local'), split_axis=0, concat_axis=0,...]
  transfers between devices with their start and end apart: 1 -> 1, of which waited for: 1 -> 1; matrix products, arithmetic and copies ran while one was open for 1% -> 2% of each run, Pallas kernels for 0% -> 0%
where the time goes in v1:
time: 390 us; the launch traced here: 387 us
  blocking collectives  115 us (29%)
  local copies, waits for them, and re-layouts  109 us (28%)
  waiting for transfers between devices  101 us (26%)
  matrix products  41.5 us (11%)
  other arithmetic  12.9 us (3%)
  starting transfers between devices  8.08 us (2%)
    all_to_all x1, blocking collectives, on_device(): lax.all_to_all(send_rows, ('node', 'local'), split_axis=0, concat_axis=0,...  115 us
    all_to_all x1, waiting for transfers between devices, on_device(): lax.all_to_all(produced, ('node', 'local'), split_axis=0, concat_axis=0,...  101 us
    gather x1, local copies, waits for them, and re-layouts, on_device(): returned.reshape(-1, feat_width)[slot_index]  18.6 us
    reshape x1, local copies, waits for them, and re-layouts, on_device(): fill_slots(tokens, owners, slot_index, experts_all * cap_rows).reshape(wire)  17.6 us
    reshape x1, local copies, waits for them, and re-layouts, on_device(): expert_rows(received.reshape(-1, feat_width), w_gate, w_up, w_down)  17.6 us
    reshape x1, local copies, waits for them, and re-layouts, on_device(): received.reshape(-1, feat_width)  16.9 us
    reshape x1, local copies, waits for them, and re-layouts, on_device(): returned.reshape(-1, feat_width)[slot_index]  16.9 us
    dot_general x1, matrix products, expert_rows(): jnp.dot(hidden, w_down[0], preferred_element_type=jnp.float32)  14.9 us
  transfers between devices with their start and end apart: 1, of which 1 were waited for; matrix products, arithmetic and copies ran while one was open for 2% of the time, Pallas kernels for 0%

profile of v1, /device:TPU:14, one launch (start us, length us, event | category | flops | bytes accessed | tf_op | source)
XLA Modules:
  0.0 386.9 jit_solution(7631465303720410089)
XLA Ops:
  0.0 0.8 broadcast_multiply_fusion.1
  0.8 0.7 bitcast_or_fusion
  1.5 0.1 copy.17
  1.6 0.1 eq.29
  1.7 0.1 eq.25
  1.8 0.1 copy.19
  1.9 0.2 fusion.13
  2.2 0.1 copy.20
  2.3 0.1 copy.16
  2.4 0.1 mul.60
  2.5 0.4 fusion.12
  2.9 4.3 %scatter_custom_fusion = s32[1280]{0:T(1024)S(1)} fusion(s32[1024]{0:T(1024)S(1)} %bitcast.37, s32[1024]{0:T(1024)S(1)} %add_select_fusion, s32[]{:T(128)} %constant.31.clone.1), kind=kCustom, calls=%fused_computation.38 | custom fusion | bytes 5124 | tf_op jit(solution)/shard_map/scatter | solution.py:16
  7.2 1.2 concatenate.3
  8.5 7.9 %gather_fusion = bf16[1280,3584]{1,0:T(8,128)(2,1)} fusion(bf16[129,3584]{1,0:T(8,128)(2,1)S(1)} %concatenate.3, s32[2048]{0:T(1024)S(1)} %pad_clamp_fusion), kind=kCustom, calls=%fused_computation | custom fusion | bytes 18355200 | tf_op jit(solution)/shard_map/gather | solution.py:20
  16.3 17.6 %reshape.87 = bf16[128,280,128]{2,1,0:T(8,128)(2,1)} reshape(bf16[1280,3584]{1,0:T(8,128)(2,1)} %gather_fusion) | data formatting | bytes 18350080 | tf_op jit(solution)/shard_map/reshape | solution.py:46
  34.0 114.5 %all_to_all.10 = bf16[128,280,128]{2,1,0:T(8,128)(2,1)} all-to-all(bf16[128,280,128]{2,1,0:T(8,128)(2,1)} %reshape.87), channel_id=1, replica_groups=mesh['node'=4,'local'=32] {'node','local'}, dimensions={0} | all-to-all | bytes 18350080 | tf_op jit(solution)/shard_map/all_to_all | solution.py:47
  148.5 16.9 %reshape.88 = bf16[1280,3584]{1,0:T(8,128)(2,1)} reshape(bf16[128,280,128]{2,1,0:T(8,128)(2,1)} %all_to_all.10) | data formatting | bytes 18350080 | tf_op jit(solution)/shard_map/reshape | solution.py:48
  165.4 13.4 %fusion.2 = f32[1280,1024]{1,0:T(8,128)S(1)} fusion(bf16[1280,3584]{1,0:T(8,128)(2,1)} %reshape.88, bf16[1,3584,1024]{2,1,0:T(8,128)(2,1)} %param.12), kind=kOutput, calls=%fused_computation.8 | convolution fusion | flops 9395240960 | bytes 21757952 | tf_op jit(solution)/shard_map/dot_general | solution.py:25
  178.8 12.7 %multiply_convert_fusion = bf16[1280,1024]{1,0:T(8,128)(2,1)S(1)} fusion(f32[1280,1024]{1,0:T(8,128)S(1)} %fusion.2, bf16[1280,3584]{1,0:T(8,128)(2,1)S(1)} %copy-done.1, bf16[1,3584,1024]{2,1,0:T(8,128)(2,1)} %param.11), kind=kOutput, calls=%fused_computation.12 | convolution fusion | flops 9403105280 | bytes 24379392 | tf_op jit(solution)/shard_map/dot_general | solution.py:24
  191.6 14.9 %convolution_convert_fusion = bf16[1280,3584]{1,0:T(8,128)(2,1)} fusion(bf16[1280,1024]{1,0:T(8,128)(2,1)S(1)} %multiply_convert_fusion, bf16[1,1024,3584]{2,1,0:T(8,128)(2,1)} %param.13), kind=kOutput, calls=%fused_computation.4 | convolution fusion | flops 9399828480 | bytes 19136512 | tf_op jit(solution)/shard_map/dot_general | solution.py:27
  206.5 17.6 %reshape.89 = bf16[128,280,128]{2,1,0:T(8,128)(2,1)} reshape(bf16[1280,3584]{1,0:T(8,128)(2,1)} %convolution_convert_fusion) | data formatting | bytes 18350080 | tf_op jit(solution)/shard_map/reshape | solution.py:48
  224.1 8.1 %all-to-all-start.1 = ((bf16[128,280,128]{2,1,0:T(8,128)(2,1)}), bf16[128,280,128]{2,1,0:T(8,128)(2,1)}, u32[]{:S(2)}, u32[]{:S(2)}) async-start(bf16[128,280,128]{2,1,0:T(8,128)(2,1)} %reshape.89), calls=%async_computation.1 | async-start | bytes 18350080 | tf_op jit(solution)/shard_map/all_to_all | solution.py:49
  232.2 0.1 copy.13
  232.3 0.1 reshape.108
  232.4 0.4 fusion.10
  232.8 6.8 %gather_fusion.2 = f32[1024]{0:T(1024)S(1)} fusion(f32[128,128]{1,0:T(8,128)S(1)} %fusion.10, s32[1024]{0:T(1024)S(1)} %reshape.108), kind=kCustom, calls=%fused_computation.2 | custom fusion | bytes 16384 | tf_op jit(solution)/shard_map/jit(take_along_axis)/gather | solution.py:40
  239.6 0.1 reshape.111
  239.8 0.1 copy.15
  239.9 100.8 %all-to-all-done.1 = bf16[128,280,128]{2,1,0:T(8,128)(2,1)} async-done(((bf16[128,280,128]{2,1,0:T(8,128)(2,1)}), bf16[128,280,128]{2,1,0:T(8,128)(2,1)}, u32[]{:S(2)}, u32[]{:S(2)}) %all-to-all-start.1) | async-done | bytes 9175072 | tf_op jit(solution)/shard_map/all_to_all | solution.py:49
  340.8 16.9 %reshape.90 = bf16[1280,3584]{1,0:T(8,128)(2,1)} reshape(bf16[128,280,128]{2,1,0:T(8,128)(2,1)} %all-to-all-done.1) | data formatting | bytes 18350080 | tf_op jit(solution)/shard_map/reshape | solution.py:50
  357.6 18.6 %gather_fusion.1 = bf16[1024,3584]{1,0:T(8,128)(2,1)} fusion(bf16[1280,3584]{1,0:T(8,128)(2,1)} %reshape.90, s32[1024]{0:T(1024)S(1)} %broadcast_clamp_fusion), kind=kCustom, calls=%fused_computation.1 | custom fusion | bytes 14684160 | tf_op jit(solution)/shard_map/gather | solution.py:50
  376.2 10.7 %fusion = bf16[128,3584]{1,0:T(8,128)(2,1)} fusion(bf16[1024,3584]{1,0:T(8,128)(2,1)} %gather_fusion.1, f32[128,8]{1,0:T(8,128)S(1)} %copy.15), kind=kLoop, calls=%fused_computation.6 | loop fusion | flops 10551296 | bytes 8261632 | tf_op jit(solution)/shard_map/reduce_sum | solution.py:52
  (20 shorter events, 0.2 us)
Async XLA Ops:
  0.0 232.4 %copy-start = (bf16[3584,128]{1,0:T(8,128)(2,1)S(1)}, bf16[3584,128]{1,0:T(8,128)(2,1)}, u32[]{:S(2)}) copy-start(bf16[3584,128]{1,0:T(8,128)(2,1)} %param.10) | copy-start | bytes 2752516
  165.4 13.5 %copy-start.1 = (bf16[1280,3584]{1,0:T(8,128)(2,1)S(1)}, bf16[1280,3584]{1,0:T(8,128)(2,1)}, u32[]{:S(2)}) copy-start(bf16[1280,3584]{1,0:T(8,128)(2,1)} %reshape.88) | copy-start | bytes 27525124
  224.1 8.3 %copy-start.2 = (bf16[128,3584]{1,0:T(8,128)(2,1)S(1)}, bf16[128,3584]{1,0:T(8,128)(2,1)}, u32[]{:S(2)}) copy-start(bf16[128,3584]{1,0:T(8,128)(2,1)} %param.7) | copy-start | bytes 2752516
  224.1 116.7 %all-to-all-start.1 = ((bf16[128,280,128]{2,1,0:T(8,128)(2,1)}), bf16[128,280,128]{2,1,0:T(8,128)(2,1)}, u32[]{:S(2)}, u32[]{:S(2)}) async-start(bf16[128,280,128]{2,1,0:T(8,128)(2,1)} %reshape.89), calls=%async_computation.1 | async-start | bytes 18350080 | tf_op jit(solution)/shard_map/all_to_all | solution.py:49
